TPU v7x, 128 devices: a whole 4x4x4 slice. The times are simulated.
128 devices in a mesh: head: 4 (over z), page: 32 (over x, y, core).
Axes of the slice: x: 4, y: 4, z: 4, core: 2. Of those that a mesh axis runs over, the one named last changes fastest.
Arguments:
- hidden_in: bfloat16 [32, 1024, 1024], P('page', 'head'), may hold values from -6 to 6
- norm_gain: float32 [1024], replicated, may hold values from 0.1 to 1.9
- w_qkv: bfloat16 [1024, 3, 1024], P(None, None, 'head'), may hold values from -0.1875 to 0.1875
- w_out: bfloat16 [1024, 1024], P('head'), may hold values from -0.75 to 0.75
- cache_kv: bfloat16 [2, 64, 128, 1024], P(None, 'page', None, 'head'), may hold values from -110 to 110, as said below
- page_node: int32 [64], replicated, may hold values from 0 to 18, as said below
- page_fill: int32 [64], replicated, may hold values from 1 to 128
- node_parent: int32 [19], replicated, may hold values from 0 to 2, as said below
- tok_seg: int32 [32, 1024], P('page'), may hold values from 0 to 7, never falling along the last dimension, each value on 1 to 256 neighbouring positions
- req_leaf: int32 [32, 8], P('page'), may hold values from 3 to 18, as said below
Outputs:
- attn_out: bfloat16 [32, 1024, 1024], P('page', 'head')
Inputs may be any that keep to these rules, and one draw needn't show every extreme that they name: `cache_kv`: entries of the cache; keys and values. `page_node`: every node owns at least one page. `node_parent`: node 0 is the root and its own parent; nodes 1 to 2 have parent 0; the others have a parent among nodes 1 to 2, and each of those has a child. `req_leaf`: each request names a lowest-level node; every lowest-level node is named by some request.
All inputs are finite; a program needn't handle non-finite values.
Results may differ from a plain program's by a relative error of at most 0.018.
Values may be sent and summed in bfloat16 or wider, within the bound.
No kernel may reach another device: no remote copies, remote signals or barrier semaphores. Data moves between devices by JAX's collectives and lax.ppermute only.
A program may use at most 64 MiB of HBM per device.

v0:
```python
import math
import jax
import jax.numpy as jnp
from jax import lax
from jax.sharding import PartitionSpec as P

HD = 64
EPSILON = 1e-06
FLOOR_SCORE = -1e30


def lookup(indices, lookup_table):
    matches = indices[:, None] == jnp.arange(lookup_table.shape[0], dtype=jnp.int32)[None, :]
    return jnp.sum(jnp.where(matches, lookup_table[None, :], 0), axis=1)


def shards(
    hidden_in,
    norm_gain,
    w_qkv,
    w_out,
    cache_kv,
    page_node,
    page_fill,
    node_parent,
    tok_seg,
    req_leaf,
):
    widened = hidden_in[0].astype(jnp.float32)
    normed = (
        widened
        * lax.rsqrt(jnp.mean(widened * widened, axis=1, keepdims=True) + EPSILON)
        * norm_gain
    ).astype(jnp.bfloat16)
    model_width = widened.shape[1]
    group_width = w_qkv.shape[2]
    head_size = HD
    group_heads = group_width // head_size
    weight_flat = w_qkv.reshape(model_width, 3 * group_width)
    projected = jnp.dot(
        lax.all_gather(normed, "head", axis=0, tiled=True),
        weight_flat,
        preferred_element_type=jnp.float32,
    ).astype(jnp.bfloat16)
    queries_all = projected.shape[0]
    queries = projected[:, :group_width].reshape(queries_all, group_heads, head_size)
    key_new = projected[:, group_width : 2 * group_width].reshape(
        queries_all, group_heads, head_size
    )
    value_new = projected[:, 2 * group_width :].reshape(queries_all, group_heads, head_size)
    score_scale = head_size ** (-0.5)
    segment = tok_seg[0]
    leaf_node = lookup(segment, req_leaf[0])
    upper_node = lookup(leaf_node, node_parent)
    root_node = lookup(upper_node, node_parent)
    position = jnp.arange(queries_all, dtype=jnp.int32)
    block_rows = min(queries_all, 512)

    def suffix_block(first):
        query_rows = lax.dynamic_slice_in_dim(queries, first, block_rows, 0)
        segment_rows = lax.dynamic_slice_in_dim(segment, first, block_rows, 0)
        position_rows = first + jnp.arange(block_rows, dtype=jnp.int32)
        visible = (segment_rows[:, None] == segment[None, :]) & (
            position[None, :] <= position_rows[:, None]
        )
        scores = (
            jnp.einsum("qhd,khd->hqk", query_rows, key_new, preferred_element_type=jnp.float32)
            * score_scale
        )
        scores = jnp.where(visible[None], scores, FLOOR_SCORE)
        row_max = jnp.max(scores, axis=2)
        weights = jnp.where(visible[None], jnp.exp(scores - row_max[:, :, None]), 0.0)
        row_sum = jnp.sum(weights, axis=2)
        weighted = jnp.einsum(
            "hqk,khd->hqd",
            weights.astype(jnp.bfloat16),
            value_new,
            preferred_element_type=jnp.float32,
        )
        return (row_max, row_sum, weighted)

    block_starts = jnp.arange(0, queries_all, block_rows, dtype=jnp.int32)
    block_max, block_sum, block_weighted = lax.map(suffix_block, block_starts)
    initial = (
        jnp.transpose(block_max, (1, 0, 2)).reshape(group_heads, queries_all),
        jnp.transpose(block_sum, (1, 0, 2)).reshape(group_heads, queries_all),
        jnp.transpose(block_weighted, (1, 0, 2, 3)).reshape(group_heads, queries_all, head_size),
    )
    page_len = cache_kv.shape[2]
    page_slot = jnp.arange(page_len, dtype=jnp.int32)
    shard_piece = lax.all_gather(cache_kv, "page", axis=1, tiled=True)
    piece_pages = shard_piece.shape[1]
    group_pages = math.gcd(piece_pages, 4)
    step_count = piece_pages // group_pages
    block_keys = group_pages * page_len
    key_blocks = shard_piece[0].reshape(step_count, block_keys, group_heads, head_size)
    value_blocks = shard_piece[1].reshape(step_count, block_keys, group_heads, head_size)
    key_nodes = jnp.repeat(page_node, page_len).reshape(step_count, block_keys)
    key_valid = (page_slot[None, :] < page_fill[:, None]).reshape(step_count, block_keys)

    def one_step(partial_value, inputs):
        row_max, row_sum, weighted = partial_value
        key_block, value_block, node_block, valid_block = inputs
        visible = (
            (node_block[None, :] == leaf_node[:, None])
            | (node_block[None, :] == upper_node[:, None])
            | (node_block[None, :] == root_node[:, None])
        ) & valid_block[None, :]
        scores = (
            jnp.einsum("qhd,khd->hqk", queries, key_block, preferred_element_type=jnp.float32)
            * score_scale
        )
        scores = jnp.where(visible[None], scores, FLOOR_SCORE)
        new_max = jnp.maximum(row_max, jnp.max(scores, axis=2))
        rescale = jnp.exp(row_max - new_max)
        weights = jnp.where(visible[None], jnp.exp(scores - new_max[:, :, None]), 0.0)
        row_sum = row_sum * rescale + jnp.sum(weights, axis=2)
        weighted = weighted * rescale[:, :, None] + jnp.einsum(
            "hqk,khd->hqd",
            weights.astype(jnp.bfloat16),
            value_block,
            preferred_element_type=jnp.float32,
        )
        return ((new_max, row_sum, weighted), None)

    result_state, unused = lax.scan(
        one_step, initial, (key_blocks, value_blocks, key_nodes, key_valid)
    )
    final_max, final_sum, final_weighted = result_state
    attention = (final_weighted / final_sum[:, :, None]).astype(jnp.bfloat16)
    attention = jnp.transpose(attention, (1, 0, 2)).reshape(queries_all, group_width)
    result = lax.psum_scatter(
        jnp.dot(attention, w_out, preferred_element_type=jnp.float32).astype(jnp.bfloat16),
        "head",
        scatter_dimension=0,
        tiled=True,
    )
    return result[None]


def solution(mesh):
    placed = (
        P("page", "head", None),
        P(),
        P(None, None, "head"),
        P("head", None),
        P(None, "page", None, "head"),
        P(),
        P(),
        P(),
        P("page", None),
        P("page", None),
    )
    return jax.shard_map(
        shards, mesh=mesh, in_specs=placed, out_specs=P("page", "head", None), check_vma=False
    )
```

profile of v0, /device:TPU:1, one launch (start us, length us, event | category | flops | bytes accessed | tf_op | source)
XLA Modules:
  0.0 339.6 jit_solution(15440758614901769843)
XLA Ops:
  16.4 27.6 %all-gather.3.cloned.1.call-done = bf16[1024,1024]{1,0:T(8,128)(2,1)} async-done(((bf16[256,1024]{1,0:T(8,128)(2,1)}), bf16[1024,1024]{1,0:T(8,128)(2,1)}) %all-gather.3.cloned.1.call-update) | async-done | bytes 2097168 | tf_op jit(solution)/shard_map/all_gather | solution.py:41
  44.1 3.4 %convolution_convert_fusion.1 = bf16[1024,768]{0,1:T(8,128)(2,1)S(1)} fusion(bf16[1024,1024]{1,0:T(8,128)(2,1)} %all-gather.3.cloned.1.call-done, bf16[1024,768]{0,1:T(8,128)(2,1)S(1)} %bitcast.106), kind=kOutput, calls=%fused_computation.45 | convolution fusion | flops 1611399168 | bytes 5242880 | tf_op jit(solution)/shard_map/dot_general | solution.py:40
  48.4 24.0 %while.30 = (s32[]{:T(128)}, f32[2,4,512]{2,1,0:T(4,128)S(1)}, f32[2,4,512]{2,1,0:T(4,128)S(1)}, f32[2,4,512,64]{2,3,1,0:T(8,128)S(1)}, s32[2]{0:T(128)S(1)}, /*...) while((s32[]{:T(128)}, f32[2,4,512]{2,1,0:T(4,128)S(1)}, ...), condition=%wide.region_4.5_spmd.clone, body=%wide.region_1.4_spmd.clone.sunk | while | flops 565703168 | bytes 29178048 | solution.py:83
  53.9 3.5 %fusion.77 = f32[2,4,512,64]{2,3,1,0:T(8,128)S(1)} fusion(f32[2,4,512,64]{2,3,1,0:T(8,128)S(1)} %get-tuple-element.401, s32[]{:T(128)} %get-tuple-element.398, bf16[1024,4,64]{0,2,1:T(8,128)(2,1)} %get-tuple-element.420, f32[4,512,1024]{2,1,0:T(8,128)S(1)} %get-tuple-element.381, f32[4,512]{1,0:T(4,128)S(1)} %get-tuple-element.382, ...), kind=kOutput, calls=%fused_computation.11.clone.1 | convolution fusion | flops 278921216 | bytes 9969668 | tf_op jit(solution)/shard_map/while/body/eval_jaxpr/hqk,khd->hqd/dot_general | solution.py:74
  57.4 2.9 fusion.76
  65.9 3.5 %fusion.77 = f32[2,4,512,64]{2,3,1,0:T(8,128)S(1)} fusion(f32[2,4,512,64]{2,3,1,0:T(8,128)S(1)} %get-tuple-element.401, s32[]{:T(128)} %get-tuple-element.398, bf16[1024,4,64]{0,2,1:T(8,128)(2,1)} %get-tuple-element.420, f32[4,512,1024]{2,1,0:T(8,128)S(1)} %get-tuple-element.381, f32[4,512]{1,0:T(4,128)S(1)} %get-tuple-element.382, ...), kind=kOutput, calls=%fused_computation.11.clone.1 | convolution fusion | flops 278921216 | bytes 9969668 | tf_op jit(solution)/shard_map/while/body/eval_jaxpr/hqk,khd->hqd/dot_general | solution.py:74
  69.4 2.9 fusion.76
  72.5 27.1 %all-gather.5.cloned.1.call-done = bf16[2,64,128,256]{3,2,1,0:T(8,128)(2,1)} async-done(((bf16[2,2,128,256]{3,2,1,0:T(8,128)(2,1)}), bf16[2,64,128,256]{3,2,1,0:T(8,128)(2,1)}) %all-gather.5.cloned.1.call-update) | async-done | bytes 8388624 | tf_op jit(solution)/shard_map/all_gather | solution.py:91
  99.5 6.0 %fusion.43 = (bf16[1,64,128,256]{3,2,1,0:T(8,128)(2,1)}, bf16[1,64,128,256]{3,2,1,0:T(8,128)(2,1)}) fusion(bf16[2,64,128,256]{3,2,1,0:T(8,128)(2,1)} %all-gather.5.cloned.1.call-done), kind=kLoop, calls=%fused_computation.63 | loop fusion | bytes 16777216 | tf_op jit(solution)/shard_map/slice | solution.py:97
  105.5 12.9 %reshape.224 = bf16[16,512,4,64]{3,2,1,0:T(4,128)(2,1)} reshape(bf16[1,64,128,256]{3,2,1,0:T(8,128)(2,1)} %get-tuple-element.231) | data formatting | bytes 8388608 | tf_op jit(solution)/shard_map/reshape;squeeze | solution.py:96
  118.4 12.7 %copy.24 = bf16[16,512,4,64]{1,3,2,0:T(8,128)(2,1)} copy(bf16[16,512,4,64]{3,2,1,0:T(4,128)(2,1)} %reshape.224) | data formatting | bytes 8388608 | tf_op jit(solution)/shard_map/while | solution.py:126
  131.1 12.9 %reshape.225 = bf16[16,512,4,64]{3,2,1,0:T(4,128)(2,1)} reshape(bf16[1,64,128,256]{3,2,1,0:T(8,128)(2,1)} %get-tuple-element.230) | data formatting | bytes 8388608 | tf_op jit(solution)/shard_map/reshape;squeeze | solution.py:97
  144.0 12.7 %copy.25 = bf16[16,512,4,64]{1,3,2,0:T(8,128)(2,1)} copy(bf16[16,512,4,64]{3,2,1,0:T(4,128)(2,1)} %reshape.225) | data formatting | bytes 8388608 | tf_op jit(solution)/shard_map/while | solution.py:126
  156.7 145.0 %while.29 = (s32[]{:T(128)}, f32[4,1024]{1,0:T(4,128)S(1)}, f32[4,1024]{1,0:T(4,128)S(1)}, f32[4,1024,64]{1,2,0:T(8,128)S(1)}, s32[16,512]{1,0:T(8,128)S(1)}, /*...) while((s32[]{:T(128)}, f32[4,1024]{1,0:T(4,128)S(1)}, ...), condition=%wide.region_11.12_spmd, body=%wide.region_8.11_spmd.sunk | while | flops 567812096 | bytes 30691972 | solution.py:126
  157.3 2.6 fusion.68
  159.9 2.1 fusion.69
  162.0 3.6 %fusion.70 = f32[4,1024,64]{1,2,0:T(8,128)S(1)} fusion(f32[4,512,1024]{2,1,0:T(8,128)S(1)} %get-tuple-element.368, f32[4,1024]{1,0:T(4,128)S(1)} %max.4, pred[1024,512]{0,1:T(8,128)(4,1)S(1)} %or_and_fusion.2, f32[4,1024,64]{1,2,0:T(8,128)S(1)} %get-tuple-element.440, f32[4,1024]{1,0:T(4,128)S(1)} %get-tuple-element.370, ...), kind=kOutput, calls=%fused_computation.29.clone.1 | convolution fusion | flops 279445504 | bytes 11305472 | tf_op jit(solution)/shard_map/while/body/eval_jaxpr/hqk,khd->hqd/dot_general | solution.py:118
  166.4 2.6 fusion.68
  171.1 3.6 %fusion.70 = f32[4,1024,64]{1,2,0:T(8,128)S(1)} fusion(f32[4,512,1024]{2,1,0:T(8,128)S(1)} %get-tuple-element.368, f32[4,1024]{1,0:T(4,128)S(1)} %max.4, pred[1024,512]{0,1:T(8,128)(4,1)S(1)} %or_and_fusion.2, f32[4,1024,64]{1,2,0:T(8,128)S(1)} %get-tuple-element.440, f32[4,1024]{1,0:T(4,128)S(1)} %get-tuple-element.370, ...), kind=kOutput, calls=%fused_computation.29.clone.1 | convolution fusion | flops 279445504 | bytes 11305472 | tf_op jit(solution)/shard_map/while/body/eval_jaxpr/hqk,khd->hqd/dot_general | solution.py:118
  175.5 2.6 fusion.68
  180.2 3.6 %fusion.70 = f32[4,1024,64]{1,2,0:T(8,128)S(1)} fusion(f32[4,512,1024]{2,1,0:T(8,128)S(1)} %get-tuple-element.368, f32[4,1024]{1,0:T(4,128)S(1)} %max.4, pred[1024,512]{0,1:T(8,128)(4,1)S(1)} %or_and_fusion.2, f32[4,1024,64]{1,2,0:T(8,128)S(1)} %get-tuple-element.440, f32[4,1024]{1,0:T(4,128)S(1)} %get-tuple-element.370, ...), kind=kOutput, calls=%fused_computation.29.clone.1 | convolution fusion | flops 279445504 | bytes 11305472 | tf_op jit(solution)/shard_map/while/body/eval_jaxpr/hqk,khd->hqd/dot_general | solution.py:118
  184.5 2.6 fusion.68
  189.2 3.6 %fusion.70 = f32[4,1024,64]{1,2,0:T(8,128)S(1)} fusion(f32[4,512,1024]{2,1,0:T(8,128)S(1)} %get-tuple-element.368, f32[4,1024]{1,0:T(4,128)S(1)} %max.4, pred[1024,512]{0,1:T(8,128)(4,1)S(1)} %or_and_fusion.2, f32[4,1024,64]{1,2,0:T(8,128)S(1)} %get-tuple-element.440, f32[4,1024]{1,0:T(4,128)S(1)} %get-tuple-element.370, ...), kind=kOutput, calls=%fused_computation.29.clone.1 | convolution fusion | flops 279445504 | bytes 11305472 | tf_op jit(solution)/shard_map/while/body/eval_jaxpr/hqk,khd->hqd/dot_general | solution.py:118
  193.6 2.6 fusion.68
  198.3 3.6 %fusion.70 = f32[4,1024,64]{1,2,0:T(8,128)S(1)} fusion(f32[4,512,1024]{2,1,0:T(8,128)S(1)} %get-tuple-element.368, f32[4,1024]{1,0:T(4,128)S(1)} %max.4, pred[1024,512]{0,1:T(8,128)(4,1)S(1)} %or_and_fusion.2, f32[4,1024,64]{1,2,0:T(8,128)S(1)} %get-tuple-element.440, f32[4,1024]{1,0:T(4,128)S(1)} %get-tuple-element.370, ...), kind=kOutput, calls=%fused_computation.29.clone.1 | convolution fusion | flops 279445504 | bytes 11305472 | tf_op jit(solution)/shard_map/while/body/eval_jaxpr/hqk,khd->hqd/dot_general | solution.py:118
  202.6 2.6 fusion.68
  207.4 3.6 %fusion.70 = f32[4,1024,64]{1,2,0:T(8,128)S(1)} fusion(f32[4,512,1024]{2,1,0:T(8,128)S(1)} %get-tuple-element.368, f32[4,1024]{1,0:T(4,128)S(1)} %max.4, pred[1024,512]{0,1:T(8,128)(4,1)S(1)} %or_and_fusion.2, f32[4,1024,64]{1,2,0:T(8,128)S(1)} %get-tuple-element.440, f32[4,1024]{1,0:T(4,128)S(1)} %get-tuple-element.370, ...), kind=kOutput, calls=%fused_computation.29.clone.1 | convolution fusion | flops 279445504 | bytes 11305472 | tf_op jit(solution)/shard_map/while/body/eval_jaxpr/hqk,khd->hqd/dot_general | solution.py:118
  211.7 2.6 fusion.68
  216.4 3.6 %fusion.70 = f32[4,1024,64]{1,2,0:T(8,128)S(1)} fusion(f32[4,512,1024]{2,1,0:T(8,128)S(1)} %get-tuple-element.368, f32[4,1024]{1,0:T(4,128)S(1)} %max.4, pred[1024,512]{0,1:T(8,128)(4,1)S(1)} %or_and_fusion.2, f32[4,1024,64]{1,2,0:T(8,128)S(1)} %get-tuple-element.440, f32[4,1024]{1,0:T(4,128)S(1)} %get-tuple-element.370, ...), kind=kOutput, calls=%fused_computation.29.clone.1 | convolution fusion | flops 279445504 | bytes 11305472 | tf_op jit(solution)/shard_map/while/body/eval_jaxpr/hqk,khd->hqd/dot_general | solution.py:118
  220.8 2.6 fusion.68
  225.5 3.6 %fusion.70 = f32[4,1024,64]{1,2,0:T(8,128)S(1)} fusion(f32[4,512,1024]{2,1,0:T(8,128)S(1)} %get-tuple-element.368, f32[4,1024]{1,0:T(4,128)S(1)} %max.4, pred[1024,512]{0,1:T(8,128)(4,1)S(1)} %or_and_fusion.2, f32[4,1024,64]{1,2,0:T(8,128)S(1)} %get-tuple-element.440, f32[4,1024]{1,0:T(4,128)S(1)} %get-tuple-element.370, ...), kind=kOutput, calls=%fused_computation.29.clone.1 | convolution fusion | flops 279445504 | bytes 11305472 | tf_op jit(solution)/shard_map/while/body/eval_jaxpr/hqk,khd->hqd/dot_general | solution.py:118
  229.8 2.6 fusion.68
  234.5 3.6 %fusion.70 = f32[4,1024,64]{1,2,0:T(8,128)S(1)} fusion(f32[4,512,1024]{2,1,0:T(8,128)S(1)} %get-tuple-element.368, f32[4,1024]{1,0:T(4,128)S(1)} %max.4, pred[1024,512]{0,1:T(8,128)(4,1)S(1)} %or_and_fusion.2, f32[4,1024,64]{1,2,0:T(8,128)S(1)} %get-tuple-element.440, f32[4,1024]{1,0:T(4,128)S(1)} %get-tuple-element.370, ...), kind=kOutput, calls=%fused_computation.29.clone.1 | convolution fusion | flops 279445504 | bytes 11305472 | tf_op jit(solution)/shard_map/while/body/eval_jaxpr/hqk,khd->hqd/dot_general | solution.py:118
  238.9 2.6 fusion.68
  243.6 3.6 %fusion.70 = f32[4,1024,64]{1,2,0:T(8,128)S(1)} fusion(f32[4,512,1024]{2,1,0:T(8,128)S(1)} %get-tuple-element.368, f32[4,1024]{1,0:T(4,128)S(1)} %max.4, pred[1024,512]{0,1:T(8,128)(4,1)S(1)} %or_and_fusion.2, f32[4,1024,64]{1,2,0:T(8,128)S(1)} %get-tuple-element.440, f32[4,1024]{1,0:T(4,128)S(1)} %get-tuple-element.370, ...), kind=kOutput, calls=%fused_computation.29.clone.1 | convolution fusion | flops 279445504 | bytes 11305472 | tf_op jit(solution)/shard_map/while/body/eval_jaxpr/hqk,khd->hqd/dot_general | solution.py:118
  247.9 2.6 fusion.68
  252.7 3.6 %fusion.70 = f32[4,1024,64]{1,2,0:T(8,128)S(1)} fusion(f32[4,512,1024]{2,1,0:T(8,128)S(1)} %get-tuple-element.368, f32[4,1024]{1,0:T(4,128)S(1)} %max.4, pred[1024,512]{0,1:T(8,128)(4,1)S(1)} %or_and_fusion.2, f32[4,1024,64]{1,2,0:T(8,128)S(1)} %get-tuple-element.440, f32[4,1024]{1,0:T(4,128)S(1)} %get-tuple-element.370, ...), kind=kOutput, calls=%fused_computation.29.clone.1 | convolution fusion | flops 279445504 | bytes 11305472 | tf_op jit(solution)/shard_map/while/body/eval_jaxpr/hqk,khd->hqd/dot_general | solution.py:118
  257.0 2.6 fusion.68
  261.7 3.6 %fusion.70 = f32[4,1024,64]{1,2,0:T(8,128)S(1)} fusion(f32[4,512,1024]{2,1,0:T(8,128)S(1)} %get-tuple-element.368, f32[4,1024]{1,0:T(4,128)S(1)} %max.4, pred[1024,512]{0,1:T(8,128)(4,1)S(1)} %or_and_fusion.2, f32[4,1024,64]{1,2,0:T(8,128)S(1)} %get-tuple-element.440, f32[4,1024]{1,0:T(4,128)S(1)} %get-tuple-element.370, ...), kind=kOutput, calls=%fused_computation.29.clone.1 | convolution fusion | flops 279445504 | bytes 11305472 | tf_op jit(solution)/shard_map/while/body/eval_jaxpr/hqk,khd->hqd/dot_general | solution.py:118
  266.1 2.6 fusion.68
  270.8 3.6 %fusion.70 = f32[4,1024,64]{1,2,0:T(8,128)S(1)} fusion(f32[4,512,1024]{2,1,0:T(8,128)S(1)} %get-tuple-element.368, f32[4,1024]{1,0:T(4,128)S(1)} %max.4, pred[1024,512]{0,1:T(8,128)(4,1)S(1)} %or_and_fusion.2, f32[4,1024,64]{1,2,0:T(8,128)S(1)} %get-tuple-element.440, f32[4,1024]{1,0:T(4,128)S(1)} %get-tuple-element.370, ...), kind=kOutput, calls=%fused_computation.29.clone.1 | convolution fusion | flops 279445504 | bytes 11305472 | tf_op jit(solution)/shard_map/while/body/eval_jaxpr/hqk,khd->hqd/dot_general | solution.py:118
  275.1 2.6 fusion.68
  279.8 3.6 %fusion.70 = f32[4,1024,64]{1,2,0:T(8,128)S(1)} fusion(f32[4,512,1024]{2,1,0:T(8,128)S(1)} %get-tuple-element.368, f32[4,1024]{1,0:T(4,128)S(1)} %max.4, pred[1024,512]{0,1:T(8,128)(4,1)S(1)} %or_and_fusion.2, f32[4,1024,64]{1,2,0:T(8,128)S(1)} %get-tuple-element.440, f32[4,1024]{1,0:T(4,128)S(1)} %get-tuple-element.370, ...), kind=kOutput, calls=%fused_computation.29.clone.1 | convolution fusion | flops 279445504 | bytes 11305472 | tf_op jit(solution)/shard_map/while/body/eval_jaxpr/hqk,khd->hqd/dot_general | solution.py:118
  284.2 2.6 fusion.68
  288.9 3.6 %fusion.70 = f32[4,1024,64]{1,2,0:T(8,128)S(1)} fusion(f32[4,512,1024]{2,1,0:T(8,128)S(1)} %get-tuple-element.368, f32[4,1024]{1,0:T(4,128)S(1)} %max.4, pred[1024,512]{0,1:T(8,128)(4,1)S(1)} %or_and_fusion.2, f32[4,1024,64]{1,2,0:T(8,128)S(1)} %get-tuple-element.440, f32[4,1024]{1,0:T(4,128)S(1)} %get-tuple-element.370, ...), kind=kOutput, calls=%fused_computation.29.clone.1 | convolution fusion | flops 279445504 | bytes 11305472 | tf_op jit(solution)/shard_map/while/body/eval_jaxpr/hqk,khd->hqd/dot_general | solution.py:118
  293.3 2.6 fusion.68
  298.0 3.6 %fusion.70 = f32[4,1024,64]{1,2,0:T(8,128)S(1)} fusion(f32[4,512,1024]{2,1,0:T(8,128)S(1)} %get-tuple-element.368, f32[4,1024]{1,0:T(4,128)S(1)} %max.4, pred[1024,512]{0,1:T(8,128)(4,1)S(1)} %or_and_fusion.2, f32[4,1024,64]{1,2,0:T(8,128)S(1)} %get-tuple-element.440, f32[4,1024]{1,0:T(4,128)S(1)} %get-tuple-element.370, ...), kind=kOutput, calls=%fused_computation.29.clone.1 | convolution fusion | flops 279445504 | bytes 11305472 | tf_op jit(solution)/shard_map/while/body/eval_jaxpr/hqk,khd->hqd/dot_general | solution.py:118
  303.9 29.2 %reduce-scatter.2.cloned.1.call-done = bf16[256,1024]{1,0:T(8,128)(2,1)} async-done(((bf16[1024,1024]{1,0:T(8,128)(2,1)}), bf16[256,1024]{1,0:T(8,128)(2,1)}) %reduce-scatter.2.cloned.1.call-update) | async-done | bytes 524304 | tf_op jit(solution)/shard_map/reduce_scatter | solution.py:132
  (155 shorter events, 63.2 us)
Async XLA Ops:
  6.5 295.2 %copy-start = (bf16[256,1024]{1,0:T(8,128)(2,1)S(1)}, bf16[256,1024]{1,0:T(8,128)(2,1)}, u32[]{:S(2)}) copy-start(bf16[256,1024]{1,0:T(8,128)(2,1)} %param.17) | copy-start | bytes 1572868
  6.5 37.5 %all-gather.3.cloned.1.call-start = ((), (), s32[]{:S(2)}) async-start(), calls=%async_computation.1 | async-start | bytes 2621440 | tf_op jit(solution)/shard_map/all_gather | solution.py:41
  9.9 89.7 %all-gather.5.cloned.1.call-start = ((), (), s32[]{:S(2)}) async-start(), calls=%async_computation.2 | async-start | bytes 8650752 | tf_op jit(solution)/shard_map/all_gather | solution.py:91
  10.6 322.5 %reduce-scatter.2.cloned.1.call-start = ((), (), s32[]{:S(2)}) async-start(), calls=%async_computation.3 | async-start | bytes 2621440 | tf_op jit(solution)/shard_map/reduce_scatter | solution.py:132
  10.7 37.7 %copy-start.1 = (s32[1,1024]{1,0:T(1,128)S(1)}, s32[1,1024]{1,0:T(1,128)}, u32[]{:S(2)}) copy-start(s32[1,1024]{1,0:T(1,128)} %param.22) | copy-start | bytes 12292
Sparse Core Ops, SparseCore 0:
  10.0 34.0 all-gather.2
  46.4 53.0 all-gather.4
  304.0 29.0 reduce-scatter.1
where the time goes:
time: 342 us; the launch traced here: 340 us
  matrix products  116 us (34%)
  waiting for transfers between devices  84.7 us (25%)
  local copies, waits for them, and re-layouts  63.5 us (19%)
  other arithmetic  57.9 us (17%)
  between operations  13.2 us (4%)
  loops' own time  4.56 us (1%)
    dot_general x16, matrix products, one_step(): jnp.einsum('hqk,khd->hqd', weights.astype(jnp.bfloat16), value_block, pre...  58.4 us
    dot_general x16, matrix products, one_step(): jnp.einsum('qhd,khd->hqk', queries, key_block, preferred_element_type=jnp...  40.8 us
    reduce_sum x16, other arithmetic, one_step(): row_sum = row_sum * rescale + jnp.sum(weights, axis=2)  33.7 us
    reduce_scatter x1, waiting for transfers between devices, shards(): lax.psum_scatter(jnp.dot(attention, w_out, preferred_element_type=jnp.flo...  29.2 us
    all_gather x1, waiting for transfers between devices, shards(): lax.all_gather(normed, 'head', axis=0, tiled=True)  27.6 us
    all_gather x1, waiting for transfers between devices, shards(): shard_piece = lax.all_gather(cache_kv, 'page', axis=1, tiled=True)  27.1 us
    while x2, local copies, waits for them, and re-layouts, shards(): lax.scan(one_step, initial, (key_blocks, value_blocks, key_nodes, key_val...  25.4 us
    another operation x1, local copies, waits for them, and re-layouts, shards(): shard_piece[0].reshape(step_count, block_keys, group_heads, head_size)  12.9 us
  transfers between devices with their start and end apart: 3, of which 3 were waited for; matrix products, arithmetic and copies ran while one was open for 9% of the time, Pallas kernels for 0%

commit v1 on v0

--- a/solution.py
+++ b/solution.py
@@ -7,6 +7,19 @@
 HD = 64
 EPSILON = 1e-06
 FLOOR_SCORE = -1e30
+
+
+def ring_gather(shard, axis, dim):
+    ways = lax.axis_size(axis)
+    up = [(d, (d + 1) % ways) for d in range(ways)]
+    down = [(d, (d - 1) % ways) for d in range(ways)]
+    earlier, later = ([shard], [shard])
+    for _ in range(ways // 2):
+        earlier.append(lax.ppermute(earlier[-1], axis, up))
+    for _ in range((ways - 1) // 2):
+        later.append(lax.ppermute(later[-1], axis, down))
+    line = jnp.concatenate([*earlier[::-1], *later[1:]], axis=dim)
+    return jnp.roll(line, (lax.axis_index(axis) - ways // 2) * shard.shape[dim], axis=dim)
 
 
 def lookup(indices, lookup_table):
@@ -38,9 +51,7 @@
     group_heads = group_width // head_size
     weight_flat = w_qkv.reshape(model_width, 3 * group_width)
     projected = jnp.dot(
-        lax.all_gather(normed, "head", axis=0, tiled=True),
-        weight_flat,
-        preferred_element_type=jnp.float32,
+        ring_gather(normed, "head", 0), weight_flat, preferred_element_type=jnp.float32
     ).astype(jnp.bfloat16)
     queries_all = projected.shape[0]
     queries = projected[:, :group_width].reshape(queries_all, group_heads, head_size)

time: 342 us -> 311 us (0.909)
  waiting for transfers between devices: 84.7 us -> 50 us
  starting transfers between devices: 0.08 us -> 4.8 us
    all_gather x1 -> x0, waiting for transfers between devices: 27.6 us -> none  [shards(): lax.all_gather(normed, 'head', axis=0, tiled=True)]
    all_gather x1, waiting for transfers between devices: 27.1 us -> 0.02 us  [shards(): shard_piece = lax.all_gather(cache_kv, 'page', axis=1, tiled=True)]
    ppermute x0 -> x3, waiting for transfers between devices: none -> 18.9 us  [the longest x2 18.9 us: ring_gather(): earlier.append(lax.ppermute(earlier[-1], axis, up))]
    ppermute x0 -> x3, starting transfers between devices: none -> 4.73 us  [the longest x2 2.53 us: ring_gather(): earlier.append(lax.ppermute(earlier[-1], axis, up))]
  transfers between devices with their start and end apart: 3 -> 5, of which waited for: 3 -> 3; matrix products, arithmetic and copies ran while one was open for 9% -> 10% of each run, Pallas kernels for 0% -> 0%
where the time goes in v1:
time: 311 us; the launch traced here: 309 us
  matrix products  114 us (37%)
  local copies, waits for them, and re-layouts  64.4 us (21%)
  other arithmetic  57.4 us (18%)
  waiting for transfers between devices  50 us (16%)
  between operations  13.7 us (4%)
  starting transfers between devices  4.8 us (2%)
  loops' own time  4.57 us (1%)
    dot_general x16, matrix products, one_step(): jnp.einsum('hqk,khd->hqd', weights.astype(jnp.bfloat16), value_block, pre...  58.3 us
    dot_general x16, matrix products, one_step(): jnp.einsum('qhd,khd->hqk', queries, key_block, preferred_element_type=jnp...  40.8 us
    reduce_sum x16, other arithmetic, one_step(): row_sum = row_sum * rescale + jnp.sum(weights, axis=2)  33.7 us
    reduce_scatter x1, waiting for transfers between devices, shards(): lax.psum_scatter(jnp.dot(attention, w_out, preferred_element_type=jnp.flo...  30.4 us
    while x2, local copies, waits for them, and re-layouts, shards(): lax.scan(one_step, initial, (key_blocks, value_blocks, key_nodes, key_val...  25.4 us
    ppermute x2, waiting for transfers between devices, ring_gather(): earlier.append(lax.ppermute(earlier[-1], axis, up))  18.9 us
    another operation x1, local copies, waits for them, and re-layouts, shards(): shard_piece[0].reshape(step_count, block_keys, group_heads, head_size)  12.9 us
    another operation x1, local copies, waits for them, and re-layouts, shards(): shard_piece[1].reshape(step_count, block_keys, group_heads, head_size)  12.9 us
  transfers between devices with their start and end apart: 5, of which 3 were waited for; matrix products, arithmetic and copies ran while one was open for 10% of the time, Pallas kernels for 0%

profile of v1, /device:TPU:1, one launch (start us, length us, event | category | flops | bytes accessed | tf_op | source)
XLA Modules:
  0.0 308.6 jit_solution(9293489765851568614)
XLA Ops:
  9.8 2.5 collective-permute-start
  16.8 9.3 %collective-permute-done = bf16[256,1024]{1,0:T(8,128)(2,1)S(1)} collective-permute-done((bf16[256,1024]{1,0:T(8,128)(2,1)S(1)}, bf16[256,1024]{1,0:T(8,128)(2,1)S(1)}, u32[]{:S(2)}, u32[]{:S(2)}) %collective-permute-start) | collective-permute-done | bytes 524320 | tf_op jit(solution)/shard_map/ppermute | solution.py:18
  27.0 2.7 copy.20
  29.8 9.7 %collective-permute-done.1 = bf16[256,1024]{1,0:T(8,128)(2,1)S(1)} collective-permute-done((bf16[256,1024]{1,0:T(8,128)(2,1)S(1)}, bf16[256,1024]{1,0:T(8,128)(2,1)S(1)}, u32[]{:S(2)}, u32[]{:S(2)}) %collective-permute-start.1) | collective-permute-done | bytes 524320 | tf_op jit(solution)/shard_map/ppermute | solution.py:18
  42.2 23.4 %while.30 = (s32[]{:T(128)}, f32[2,4,512]{2,1,0:T(4,128)S(1)}, f32[2,4,512]{2,1,0:T(4,128)S(1)}, f32[2,4,512,64]{2,3,1,0:T(8,128)}, s32[2]{0:T(128)S(1)}, /*inde...) while((s32[]{:T(128)}, f32[2,4,512]{2,1,0:T(4,128)S(1)}, ...), condition=%wide.region_4.5_spmd.clone, body=%wide.region_1.4_spmd.clone.sunk | while | flops 565703168 | bytes 29178556 | solution.py:94
  47.7 3.3 %fusion.82 = f32[2,4,512,64]{2,3,1,0:T(8,128)} fusion(f32[2,4,512,64]{2,3,1,0:T(8,128)} %get-tuple-element.401, s32[]{:T(128)} %get-tuple-element.398, bf16[1024,4,64]{0,2,1:T(8,128)(2,1)S(1)} %get-tuple-element.420, f32[4,512,1024]{2,1,0:T(8,128)S(1)} %get-tuple-element.381, f32[4,512]{1,0:T(4,128)S(1)} %get-tuple-element.382, ...), kind=kOutput, calls=%fused_computation.11.clone.1 | convolution fusion | flops 278921216 | bytes 9970176 | tf_op jit(solution)/shard_map/while/body/eval_jaxpr/hqk,khd->hqd/dot_general | solution.py:85
  51.0 2.9 fusion.81
  59.4 3.3 %fusion.82 = f32[2,4,512,64]{2,3,1,0:T(8,128)} fusion(f32[2,4,512,64]{2,3,1,0:T(8,128)} %get-tuple-element.401, s32[]{:T(128)} %get-tuple-element.398, bf16[1024,4,64]{0,2,1:T(8,128)(2,1)S(1)} %get-tuple-element.420, f32[4,512,1024]{2,1,0:T(8,128)S(1)} %get-tuple-element.381, f32[4,512]{1,0:T(4,128)S(1)} %get-tuple-element.382, ...), kind=kOutput, calls=%fused_computation.11.clone.1 | convolution fusion | flops 278921216 | bytes 9970176 | tf_op jit(solution)/shard_map/while/body/eval_jaxpr/hqk,khd->hqd/dot_general | solution.py:85
  62.7 2.9 fusion.81
  67.0 6.0 %fusion.49 = (bf16[1,64,128,256]{3,2,1,0:T(8,128)(2,1)}, bf16[1,64,128,256]{3,2,1,0:T(8,128)(2,1)}) fusion(bf16[2,64,128,256]{3,2,1,0:T(8,128)(2,1)} %all-gather.2.cloned.1.call-done), kind=kLoop, calls=%fused_computation.74 | loop fusion | bytes 16777216 | tf_op jit(solution)/shard_map/slice | solution.py:108
  73.0 12.9 %reshape.224 = bf16[16,512,4,64]{3,2,1,0:T(4,128)(2,1)} reshape(bf16[1,64,128,256]{3,2,1,0:T(8,128)(2,1)} %get-tuple-element.231) | data formatting | bytes 8388608 | tf_op jit(solution)/shard_map/reshape;squeeze | solution.py:107
  85.8 12.7 %copy.24 = bf16[16,512,4,64]{1,3,2,0:T(8,128)(2,1)} copy(bf16[16,512,4,64]{3,2,1,0:T(4,128)(2,1)} %reshape.224) | data formatting | bytes 8388608 | tf_op jit(solution)/shard_map/while | solution.py:137
  98.5 12.9 %reshape.225 = bf16[16,512,4,64]{3,2,1,0:T(4,128)(2,1)} reshape(bf16[1,64,128,256]{3,2,1,0:T(8,128)(2,1)} %get-tuple-element.230) | data formatting | bytes 8388608 | tf_op jit(solution)/shard_map/reshape;squeeze | solution.py:108
  111.4 12.7 %copy.25 = bf16[16,512,4,64]{1,3,2,0:T(8,128)(2,1)} copy(bf16[16,512,4,64]{3,2,1,0:T(4,128)(2,1)} %reshape.225) | data formatting | bytes 8388608 | tf_op jit(solution)/shard_map/while | solution.py:137
  124.1 145.0 %while.29 = (s32[]{:T(128)}, f32[4,1024]{1,0:T(4,128)S(1)}, f32[4,1024]{1,0:T(4,128)S(1)}, f32[4,1024,64]{1,2,0:T(8,128)S(1)}, s32[16,512]{1,0:T(8,128)S(1)}, /*...) while((s32[]{:T(128)}, f32[4,1024]{1,0:T(4,128)S(1)}, ...), condition=%wide.region_11.12_spmd, body=%wide.region_8.11_spmd.sunk | while | flops 567812096 | bytes 30691972 | solution.py:137
  124.8 2.6 fusion.73
  129.5 3.6 %fusion.75 = f32[4,1024,64]{1,2,0:T(8,128)S(1)} fusion(f32[4,512,1024]{2,1,0:T(8,128)S(1)} %get-tuple-element.368, f32[4,1024]{1,0:T(4,128)S(1)} %max.4, pred[1024,512]{0,1:T(8,128)(4,1)S(1)} %or_and_fusion.2, f32[4,1024,64]{1,2,0:T(8,128)S(1)} %get-tuple-element.440, f32[4,1024]{1,0:T(4,128)S(1)} %get-tuple-element.370, ...), kind=kOutput, calls=%fused_computation.29.clone.1 | convolution fusion | flops 279445504 | bytes 11305472 | tf_op jit(solution)/shard_map/while/body/eval_jaxpr/hqk,khd->hqd/dot_general | solution.py:129
  133.8 2.6 fusion.73
  138.6 3.6 %fusion.75 = f32[4,1024,64]{1,2,0:T(8,128)S(1)} fusion(f32[4,512,1024]{2,1,0:T(8,128)S(1)} %get-tuple-element.368, f32[4,1024]{1,0:T(4,128)S(1)} %max.4, pred[1024,512]{0,1:T(8,128)(4,1)S(1)} %or_and_fusion.2, f32[4,1024,64]{1,2,0:T(8,128)S(1)} %get-tuple-element.440, f32[4,1024]{1,0:T(4,128)S(1)} %get-tuple-element.370, ...), kind=kOutput, calls=%fused_computation.29.clone.1 | convolution fusion | flops 279445504 | bytes 11305472 | tf_op jit(solution)/shard_map/while/body/eval_jaxpr/hqk,khd->hqd/dot_general | solution.py:129
  142.9 2.6 fusion.73
  147.6 3.6 %fusion.75 = f32[4,1024,64]{1,2,0:T(8,128)S(1)} fusion(f32[4,512,1024]{2,1,0:T(8,128)S(1)} %get-tuple-element.368, f32[4,1024]{1,0:T(4,128)S(1)} %max.4, pred[1024,512]{0,1:T(8,128)(4,1)S(1)} %or_and_fusion.2, f32[4,1024,64]{1,2,0:T(8,128)S(1)} %get-tuple-element.440, f32[4,1024]{1,0:T(4,128)S(1)} %get-tuple-element.370, ...), kind=kOutput, calls=%fused_computation.29.clone.1 | convolution fusion | flops 279445504 | bytes 11305472 | tf_op jit(solution)/shard_map/while/body/eval_jaxpr/hqk,khd->hqd/dot_general | solution.py:129
  152.0 2.6 fusion.73
  156.7 3.6 %fusion.75 = f32[4,1024,64]{1,2,0:T(8,128)S(1)} fusion(f32[4,512,1024]{2,1,0:T(8,128)S(1)} %get-tuple-element.368, f32[4,1024]{1,0:T(4,128)S(1)} %max.4, pred[1024,512]{0,1:T(8,128)(4,1)S(1)} %or_and_fusion.2, f32[4,1024,64]{1,2,0:T(8,128)S(1)} %get-tuple-element.440, f32[4,1024]{1,0:T(4,128)S(1)} %get-tuple-element.370, ...), kind=kOutput, calls=%fused_computation.29.clone.1 | convolution fusion | flops 279445504 | bytes 11305472 | tf_op jit(solution)/shard_map/while/body/eval_jaxpr/hqk,khd->hqd/dot_general | solution.py:129
  161.0 2.6 fusion.73
  165.7 3.6 %fusion.75 = f32[4,1024,64]{1,2,0:T(8,128)S(1)} fusion(f32[4,512,1024]{2,1,0:T(8,128)S(1)} %get-tuple-element.368, f32[4,1024]{1,0:T(4,128)S(1)} %max.4, pred[1024,512]{0,1:T(8,128)(4,1)S(1)} %or_and_fusion.2, f32[4,1024,64]{1,2,0:T(8,128)S(1)} %get-tuple-element.440, f32[4,1024]{1,0:T(4,128)S(1)} %get-tuple-element.370, ...), kind=kOutput, calls=%fused_computation.29.clone.1 | convolution fusion | flops 279445504 | bytes 11305472 | tf_op jit(solution)/shard_map/while/body/eval_jaxpr/hqk,khd->hqd/dot_general | solution.py:129
  170.1 2.6 fusion.73
  174.8 3.6 %fusion.75 = f32[4,1024,64]{1,2,0:T(8,128)S(1)} fusion(f32[4,512,1024]{2,1,0:T(8,128)S(1)} %get-tuple-element.368, f32[4,1024]{1,0:T(4,128)S(1)} %max.4, pred[1024,512]{0,1:T(8,128)(4,1)S(1)} %or_and_fusion.2, f32[4,1024,64]{1,2,0:T(8,128)S(1)} %get-tuple-element.440, f32[4,1024]{1,0:T(4,128)S(1)} %get-tuple-element.370, ...), kind=kOutput, calls=%fused_computation.29.clone.1 | convolution fusion | flops 279445504 | bytes 11305472 | tf_op jit(solution)/shard_map/while/body/eval_jaxpr/hqk,khd->hqd/dot_general | solution.py:129
  179.2 2.6 fusion.73
  183.9 3.6 %fusion.75 = f32[4,1024,64]{1,2,0:T(8,128)S(1)} fusion(f32[4,512,1024]{2,1,0:T(8,128)S(1)} %get-tuple-element.368, f32[4,1024]{1,0:T(4,128)S(1)} %max.4, pred[1024,512]{0,1:T(8,128)(4,1)S(1)} %or_and_fusion.2, f32[4,1024,64]{1,2,0:T(8,128)S(1)} %get-tuple-element.440, f32[4,1024]{1,0:T(4,128)S(1)} %get-tuple-element.370, ...), kind=kOutput, calls=%fused_computation.29.clone.1 | convolution fusion | flops 279445504 | bytes 11305472 | tf_op jit(solution)/shard_map/while/body/eval_jaxpr/hqk,khd->hqd/dot_general | solution.py:129
  188.2 2.6 fusion.73
  192.9 3.6 %fusion.75 = f32[4,1024,64]{1,2,0:T(8,128)S(1)} fusion(f32[4,512,1024]{2,1,0:T(8,128)S(1)} %get-tuple-element.368, f32[4,1024]{1,0:T(4,128)S(1)} %max.4, pred[1024,512]{0,1:T(8,128)(4,1)S(1)} %or_and_fusion.2, f32[4,1024,64]{1,2,0:T(8,128)S(1)} %get-tuple-element.440, f32[4,1024]{1,0:T(4,128)S(1)} %get-tuple-element.370, ...), kind=kOutput, calls=%fused_computation.29.clone.1 | convolution fusion | flops 279445504 | bytes 11305472 | tf_op jit(solution)/shard_map/while/body/eval_jaxpr/hqk,khd->hqd/dot_general | solution.py:129
  197.3 2.6 fusion.73
  202.0 3.6 %fusion.75 = f32[4,1024,64]{1,2,0:T(8,128)S(1)} fusion(f32[4,512,1024]{2,1,0:T(8,128)S(1)} %get-tuple-element.368, f32[4,1024]{1,0:T(4,128)S(1)} %max.4, pred[1024,512]{0,1:T(8,128)(4,1)S(1)} %or_and_fusion.2, f32[4,1024,64]{1,2,0:T(8,128)S(1)} %get-tuple-element.440, f32[4,1024]{1,0:T(4,128)S(1)} %get-tuple-element.370, ...), kind=kOutput, calls=%fused_computation.29.clone.1 | convolution fusion | flops 279445504 | bytes 11305472 | tf_op jit(solution)/shard_map/while/body/eval_jaxpr/hqk,khd->hqd/dot_general | solution.py:129
  206.3 2.6 fusion.73
  211.1 3.6 %fusion.75 = f32[4,1024,64]{1,2,0:T(8,128)S(1)} fusion(f32[4,512,1024]{2,1,0:T(8,128)S(1)} %get-tuple-element.368, f32[4,1024]{1,0:T(4,128)S(1)} %max.4, pred[1024,512]{0,1:T(8,128)(4,1)S(1)} %or_and_fusion.2, f32[4,1024,64]{1,2,0:T(8,128)S(1)} %get-tuple-element.440, f32[4,1024]{1,0:T(4,128)S(1)} %get-tuple-element.370, ...), kind=kOutput, calls=%fused_computation.29.clone.1 | convolution fusion | flops 279445504 | bytes 11305472 | tf_op jit(solution)/shard_map/while/body/eval_jaxpr/hqk,khd->hqd/dot_general | solution.py:129
  215.4 2.6 fusion.73
  220.1 3.6 %fusion.75 = f32[4,1024,64]{1,2,0:T(8,128)S(1)} fusion(f32[4,512,1024]{2,1,0:T(8,128)S(1)} %get-tuple-element.368, f32[4,1024]{1,0:T(4,128)S(1)} %max.4, pred[1024,512]{0,1:T(8,128)(4,1)S(1)} %or_and_fusion.2, f32[4,1024,64]{1,2,0:T(8,128)S(1)} %get-tuple-element.440, f32[4,1024]{1,0:T(4,128)S(1)} %get-tuple-element.370, ...), kind=kOutput, calls=%fused_computation.29.clone.1 | convolution fusion | flops 279445504 | bytes 11305472 | tf_op jit(solution)/shard_map/while/body/eval_jaxpr/hqk,khd->hqd/dot_general | solution.py:129
  224.5 2.6 fusion.73
  229.2 3.6 %fusion.75 = f32[4,1024,64]{1,2,0:T(8,128)S(1)} fusion(f32[4,512,1024]{2,1,0:T(8,128)S(1)} %get-tuple-element.368, f32[4,1024]{1,0:T(4,128)S(1)} %max.4, pred[1024,512]{0,1:T(8,128)(4,1)S(1)} %or_and_fusion.2, f32[4,1024,64]{1,2,0:T(8,128)S(1)} %get-tuple-element.440, f32[4,1024]{1,0:T(4,128)S(1)} %get-tuple-element.370, ...), kind=kOutput, calls=%fused_computation.29.clone.1 | convolution fusion | flops 279445504 | bytes 11305472 | tf_op jit(solution)/shard_map/while/body/eval_jaxpr/hqk,khd->hqd/dot_general | solution.py:129
  233.5 2.6 fusion.73
  238.2 3.6 %fusion.75 = f32[4,1024,64]{1,2,0:T(8,128)S(1)} fusion(f32[4,512,1024]{2,1,0:T(8,128)S(1)} %get-tuple-element.368, f32[4,1024]{1,0:T(4,128)S(1)} %max.4, pred[1024,512]{0,1:T(8,128)(4,1)S(1)} %or_and_fusion.2, f32[4,1024,64]{1,2,0:T(8,128)S(1)} %get-tuple-element.440, f32[4,1024]{1,0:T(4,128)S(1)} %get-tuple-element.370, ...), kind=kOutput, calls=%fused_computation.29.clone.1 | convolution fusion | flops 279445504 | bytes 11305472 | tf_op jit(solution)/shard_map/while/body/eval_jaxpr/hqk,khd->hqd/dot_general | solution.py:129
  242.6 2.6 fusion.73
  247.3 3.6 %fusion.75 = f32[4,1024,64]{1,2,0:T(8,128)S(1)} fusion(f32[4,512,1024]{2,1,0:T(8,128)S(1)} %get-tuple-element.368, f32[4,1024]{1,0:T(4,128)S(1)} %max.4, pred[1024,512]{0,1:T(8,128)(4,1)S(1)} %or_and_fusion.2, f32[4,1024,64]{1,2,0:T(8,128)S(1)} %get-tuple-element.440, f32[4,1024]{1,0:T(4,128)S(1)} %get-tuple-element.370, ...), kind=kOutput, calls=%fused_computation.29.clone.1 | convolution fusion | flops 279445504 | bytes 11305472 | tf_op jit(solution)/shard_map/while/body/eval_jaxpr/hqk,khd->hqd/dot_general | solution.py:129
  251.6 2.6 fusion.73
  256.4 3.6 %fusion.75 = f32[4,1024,64]{1,2,0:T(8,128)S(1)} fusion(f32[4,512,1024]{2,1,0:T(8,128)S(1)} %get-tuple-element.368, f32[4,1024]{1,0:T(4,128)S(1)} %max.4, pred[1024,512]{0,1:T(8,128)(4,1)S(1)} %or_and_fusion.2, f32[4,1024,64]{1,2,0:T(8,128)S(1)} %get-tuple-element.440, f32[4,1024]{1,0:T(4,128)S(1)} %get-tuple-element.370, ...), kind=kOutput, calls=%fused_computation.29.clone.1 | convolution fusion | flops 279445504 | bytes 11305472 | tf_op jit(solution)/shard_map/while/body/eval_jaxpr/hqk,khd->hqd/dot_general | solution.py:129
  260.7 2.6 fusion.73
  265.4 3.6 %fusion.75 = f32[4,1024,64]{1,2,0:T(8,128)S(1)} fusion(f32[4,512,1024]{2,1,0:T(8,128)S(1)} %get-tuple-element.368, f32[4,1024]{1,0:T(4,128)S(1)} %max.4, pred[1024,512]{0,1:T(8,128)(4,1)S(1)} %or_and_fusion.2, f32[4,1024,64]{1,2,0:T(8,128)S(1)} %get-tuple-element.440, f32[4,1024]{1,0:T(4,128)S(1)} %get-tuple-element.370, ...), kind=kOutput, calls=%fused_computation.29.clone.1 | convolution fusion | flops 279445504 | bytes 11305472 | tf_op jit(solution)/shard_map/while/body/eval_jaxpr/hqk,khd->hqd/dot_general | solution.py:129
  271.3 30.4 %reduce-scatter.2.cloned.1.call-done = bf16[256,1024]{1,0:T(8,128)(2,1)} async-done(((bf16[1024,1024]{1,0:T(8,128)(2,1)}), bf16[256,1024]{1,0:T(8,128)(2,1)}) %reduce-scatter.2.cloned.1.call-update) | async-done | bytes 524304 | tf_op jit(solution)/shard_map/reduce_scatter | solution.py:143
  (174 shorter events, 67.1 us)
Async XLA Ops:
  6.5 262.7 %copy-start = (bf16[256,1024]{1,0:T(8,128)(2,1)S(1)}, bf16[256,1024]{1,0:T(8,128)(2,1)}, u32[]{:S(2)}) copy-start(bf16[256,1024]{1,0:T(8,128)(2,1)} %param.17) | copy-start | bytes 1572868
  6.5 33.1 %copy-start.1 = (bf16[1,256,1024]{2,1,0:T(8,128)(2,1)S(1)}, bf16[1,256,1024]{2,1,0:T(8,128)(2,1)}, u32[]{:S(2)}) copy-start(bf16[1,256,1024]{2,1,0:T(8,128)(2,1)} %param.14) | copy-start | bytes 1572868
  6.5 33.1 %copy-start.4 = (f32[1024]{0:T(1024)S(1)}, f32[1024]{0:T(1024)}, u32[]{:S(2)}) copy-start(f32[1024]{0:T(1024)} %param.15) | copy-start | bytes 12292
  6.5 23.1 %copy-start.5 = (s32[64]{0:T(128)S(1)}, s32[64]{0:T(128)}, u32[]{:S(2)}) copy-start(s32[64]{0:T(128)} %param.19) | copy-start | bytes 772
  6.5 60.4 %all-gather.2.cloned.1.call-start = ((), (), s32[]{:S(2)}) async-start(), calls=%async_computation.1 | async-start | bytes 8650752 | tf_op jit(solution)/shard_map/all_gather | solution.py:102
  7.3 294.4 %reduce-scatter.2.cloned.1.call-start = ((), (), s32[]{:S(2)}) async-start(), calls=%async_computation.2 | async-start | bytes 2621440 | tf_op jit(solution)/shard_map/reduce_scatter | solution.py:143
  9.8 16.3 %collective-permute-start = (bf16[256,1024]{1,0:T(8,128)(2,1)S(1)}, bf16[256,1024]{1,0:T(8,128)(2,1)S(1)}, u32[]{:S(2)}, u32[]{:S(2)}) collective-permute-start(bf16[256,1024]{1,0:T(8,128)(2,1)S(1)} %fusion.47), channel_id=1, source_target_pairs={{0,32},{32,64},{64,96},{96,0},{1,33},{33,65},{65,97},{97,1},{2,34}... | collective-permute-start | bytes 1572872 | tf_op jit(solution)/shard_map/ppermute | solution.py:18
  12.3 27.5 %collective-permute-start.2 = (bf16[256,1024]{1,0:T(8,128)(2,1)S(1)}, bf16[256,1024]{1,0:T(8,128)(2,1)S(1)}, u32[]{:S(2)}, u32[]{:S(2)}) collective-permute-start(bf16[256,1024]{1,0:T(8,128)(2,1)S(1)} %fusion.47), channel_id=1, source_target_pairs={{0,96},{32,0},{64,32},{96,64},{1,97},{33,1},{65,33},{97,65},{2,98}... | collective-permute-start | bytes 1572872 | tf_op jit(solution)/shard_map/ppermute | solution.py:20
  26.1 13.4 %collective-permute-start.1 = (bf16[256,1024]{1,0:T(8,128)(2,1)S(1)}, bf16[256,1024]{1,0:T(8,128)(2,1)S(1)}, u32[]{:S(2)}, u32[]{:S(2)}) collective-permute-start(bf16[256,1024]{1,0:T(8,128)(2,1)S(1)} %collective-permute-done), channel_id=1, source_target_pairs={{0,32},{32,64},{64,96},{96,0},{1,33},{33,65},{65,97},{97,1},{2,34}... | collective-permute-start | bytes 1572872 | tf_op jit(solution)/shard_map/ppermute | solution.py:18
  29.8 10.4 %copy-start.2 = (bf16[1024,3,256]{0,2,1:T(8,128)(2,1)S(1)}, bf16[1024,3,256]{0,2,1:T(8,128)(2,1)}, u32[]{:S(2)}) copy-start(bf16[1024,3,256]{0,2,1:T(8,128)(2,1)} %copy.20) | copy-start | bytes 4718596
  40.2 2.0 copy-start.3
Sparse Core Ops, SparseCore 0:
  9.7 56.2 all-gather.1
  271.5 30.2 reduce-scatter.1
